TPU v7x, 32 devices: a whole 2x2x4 slice. The times are simulated.
32 devices in a mesh: task: 2 (over y), row: 4 (over z), col: 4 (over x, core).
Axes of the slice: x: 2, y: 2, z: 4, core: 2. Of those that a mesh axis runs over, the one named last changes fastest.
Arguments:
- features: bfloat16 [164, 4096], P(None, ('task', 'row', 'col')), parts along dimension 1, may hold values from -6 to 6
- rung_index: int32 [4096], P(('task', 'row', 'col')), parts along dimension 0, may hold values from 0 to 3
- w_first: bfloat16 [164, 512], replicated, may hold values from -0.5 to 0.5
- b_first: float32 [512], replicated, may hold values from -4 to 4
- w_second: bfloat16 [512, 512], replicated, may hold values from -0.25 to 0.25
- b_second: float32 [512], replicated, may hold values from -4 to 4
- w_third: bfloat16 [512, 64], replicated, may hold values from -0.25 to 0.25
- targets: float32 [16, 4096], P(None, ('task', 'row', 'col')), parts along dimension 1, may hold values from -80 to 80
- fidelity_factor: float32 [8, 4], P('task'), parts along dimension 0, may hold values from -4 to 4
- inverse_scale: float32 [2], P('task'), parts along dimension 0, may hold values from 0.02 to 0.1
- noise_var: float32 [2], P('task'), parts along dimension 0, may hold values from 0.3 to 1
Outputs:
- solution: float32 [16, 4096], P(None, ('task', 'row', 'col')), parts along dimension 1
- residual: float32 [16, 4096], P(None, ('task', 'row', 'col')), parts along dimension 1
There are 2 independent parts, one for each index of `task`. A program takes and returns all parts, laid end to end along the dimension named above; an argument that names none is the same for every part. Nothing has to cross between parts.
All inputs are finite; a program needn't handle non-finite values.
Results may differ from a plain program's by a relative error of at most 0.012.
The roundings to bfloat16 on the way count: a program that leaves them out, or rounds other values in their place, can miss the bound.
Values may be sent and summed in bfloat16 or wider, within the bound.
No kernel may reach another device: no remote copies, remote signals or barrier semaphores. Data moves between devices by JAX's collectives and lax.ppermute only.
A program may use at most 64 MiB of HBM per device.

v0:
```python
import jax
import jax.numpy as jnp
from jax import lax
from jax.sharding import PartitionSpec as P

ITERS = 2


def fidelity_matrix(fidelity_factor):
    lower = jnp.tril(fidelity_factor)
    return jnp.dot(lower, lower.T, precision=lax.Precision.HIGHEST) + 0.5 * jnp.eye(
        fidelity_factor.shape[0], dtype=jnp.float32
    )


def left_product(weights, values):
    return lax.dot_general(
        weights, values, (((0,), (0,)), ((), ())), preferred_element_type=jnp.float32
    )


def outer_gram(left_side, right_side):
    return lax.dot_general(
        left_side, right_side, (((1,), (1,)), ((), ())), precision=lax.Precision.HIGHEST
    )


def solve_spd(matrix, right_side):
    return jax.scipy.linalg.cho_solve((jnp.linalg.cholesky(matrix), True), right_side)


def block_size(total_count, largest):
    chosen = min(total_count, largest)
    while total_count % chosen != 0:
        chosen = chosen - 1
    return chosen


def rung_fidelity(fidelity, rung_value):
    levels = jnp.arange(fidelity.shape[0], dtype=jnp.float32)
    onehot = (rung_value.astype(jnp.float32)[None, :] == levels[:, None]).astype(jnp.float32)
    return (jnp.dot(fidelity, onehot, precision=lax.Precision.HIGHEST), onehot)


def split_two(values):
    high = lax.reduce_precision(values, exponent_bits=8, mantissa_bits=7)
    return (high.astype(jnp.bfloat16), (values - high).astype(jnp.bfloat16))


def split_product(direction, kernel):
    count = direction.shape[0]
    d_high, d_low = split_two(direction)
    k_high, k_low = split_two(kernel)
    dims = (((1,), (1,)), ((), ()))
    by_high = lax.dot_general(
        jnp.concatenate([d_high, d_low], axis=0), k_high, dims, preferred_element_type=jnp.float32
    )
    by_low = lax.dot_general(d_high, k_low, dims, preferred_element_type=jnp.float32)
    return by_high[:count] + by_high[count:] + by_low


def kernel_image(embedding, squares, rung_onehot, col_fidelity, inverse_scale, direction):
    count = embedding.shape[1]
    row_block = block_size(count, 2048)
    col_block = block_size(count, 2048)
    levels = jnp.arange(col_fidelity.shape[0], dtype=jnp.float32)

    def one_row_block(block_number):
        first_row = block_number * row_block
        rows_embedding = lax.dynamic_slice_in_dim(embedding, first_row, row_block, 1)
        rows_squares = lax.dynamic_slice_in_dim(squares, first_row, row_block, 0)
        rows_fidelity = lax.dynamic_slice_in_dim(col_fidelity, first_row, row_block, 1)

        def one_col_block(running, column_number):
            first_col = column_number * col_block
            cols_embedding = lax.dynamic_slice_in_dim(embedding, first_col, col_block, 1)
            cols_squares = lax.dynamic_slice_in_dim(squares, first_col, col_block, 0)
            cols_fidelity = lax.dynamic_slice_in_dim(col_fidelity, first_col, col_block, 1)
            cols_direction = lax.dynamic_slice_in_dim(direction, first_col, col_block, 1)
            cols_onehot = lax.dynamic_slice_in_dim(rung_onehot, first_col, col_block, 1)
            inner = left_product(rows_embedding, cols_embedding)
            distance = rows_squares[:, None] + cols_squares[None, :] - 2.0 * inner
            radial = jnp.exp(-inverse_scale[0] * distance)
            by_rung = jnp.concatenate(
                [
                    cols_direction * cols_onehot[level][None, :]
                    for level in range(col_fidelity.shape[0])
                ],
                axis=0,
            )
            rung_products = split_product(by_rung, radial)
            rhs = direction.shape[0]
            contribution = rows_fidelity[0][None, :] * rung_products[:rhs]
            for level in range(1, col_fidelity.shape[0]):
                contribution = (
                    contribution
                    + rows_fidelity[level][None, :] * rung_products[level * rhs : (level + 1) * rhs]
                )
            return (running + contribution, None)

        start_value = jnp.zeros((direction.shape[0], row_block), jnp.float32)
        result, unused = lax.scan(
            one_col_block, start_value, jnp.arange(count // col_block, dtype=jnp.int32)
        )
        return result

    stacked = lax.map(one_row_block, jnp.arange(count // row_block, dtype=jnp.int32))
    return jnp.transpose(stacked, (1, 0, 2)).reshape(direction.shape[0], count)


def on_device(
    features,
    rung_index,
    w_first,
    b_first,
    w_second,
    b_second,
    w_third,
    targets,
    fidelity_factor,
    inverse_scale,
    noise_var,
):
    fidelity = fidelity_matrix(fidelity_factor)
    hidden_one = jax.nn.silu(left_product(w_first, features) + b_first[:, None]).astype(
        jnp.bfloat16
    )
    hidden_two = jax.nn.silu(left_product(w_second, hidden_one) + b_second[:, None]).astype(
        jnp.bfloat16
    )
    embedding = lax.reduce_precision(
        left_product(w_third, hidden_two), exponent_bits=8, mantissa_bits=7
    )
    rung_value = rung_index.astype(jnp.float32)
    own_count = targets.shape[1]
    own_first = (lax.axis_index("row") * lax.axis_size("col") + lax.axis_index("col")) * own_count
    emb_rows = embedding.shape[0]
    packed = jnp.concatenate([embedding, targets, rung_value[None, :]], axis=0)
    gathered = lax.all_gather(packed, ("row", "col"), axis=1, tiled=True)
    all_embedding = gathered[:emb_rows].astype(jnp.bfloat16)
    all_targets = gathered[emb_rows : emb_rows + targets.shape[0]]
    all_rung = gathered[emb_rows + targets.shape[0]]
    squares = jnp.sum(jnp.square(gathered[:emb_rows]), axis=0)
    col_fidelity, rung_onehot = rung_fidelity(fidelity, all_rung)
    solution = jnp.zeros_like(all_targets)
    residual = all_targets
    direction = all_targets
    gram = outer_gram(residual, residual)
    for iteration in range(ITERS):
        image = (
            kernel_image(
                all_embedding, squares, rung_onehot, col_fidelity, inverse_scale, direction
            )
            + noise_var[0] * direction
        )
        curvature = outer_gram(direction, image)
        step_matrix = solve_spd(curvature, gram)
        solution = solution + jnp.dot(step_matrix.T, direction, precision=lax.Precision.HIGHEST)
        residual = residual - jnp.dot(step_matrix.T, image, precision=lax.Precision.HIGHEST)
        if iteration + 1 < ITERS:
            new_gram = outer_gram(residual, residual)
            update_matrix = solve_spd(gram, new_gram)
            direction = residual + jnp.dot(
                update_matrix.T, direction, precision=lax.Precision.HIGHEST
            )
            gram = new_gram
    own_solution = lax.dynamic_slice_in_dim(solution, own_first, own_count, 1)
    own_residual = lax.dynamic_slice_in_dim(residual, own_first, own_count, 1)
    return (own_solution, own_residual)


def solution(mesh):
    placed = (
        P(None, ("task", "row", "col")),
        P(("task", "row", "col")),
        P(),
        P(),
        P(),
        P(),
        P(),
        P(None, ("task", "row", "col")),
        P("task", None),
        P("task"),
        P("task"),
    )
    return jax.shard_map(
        on_device,
        mesh=mesh,
        in_specs=placed,
        out_specs=(P(None, ("task", "row", "col")), P(None, ("task", "row", "col"))),
        check_vma=False,
    )
```

profile of v0, /device:TPU:0, one launch (start us, length us, event | category | flops | bytes accessed | tf_op | source)
XLA Modules:
  0.0 69.6 jit_solution(14056495379713091680)
XLA Ops:
  0.6 0.0 copy-start
  0.6 0.7 %convert_bitcast_fusion = f32[1,128]{1,0:T(1,128)S(1)} fusion(s32[128]{0:T(128)} %param.15), kind=kLoop, calls=%fused_computation.113 | loop fusion | flops 128 | bytes 1024 | tf_op jit(solution)/shard_map/broadcast_in_dim | solution.py:138
  1.4 1.2 %multiply_convert_fusion.1 = bf16[512,128]{1,0:T(8,128)(2,1)S(1)} fusion(bf16[164,512]{1,0:T(8,128)(2,1)} %param.16, bf16[164,128]{1,0:T(8,128)(2,1)} %param.14, f32[512]{0:T(512)} %param.17), kind=kOutput, calls=%fused_computation.36 | convolution fusion | flops 21889024 | bytes 343040 | tf_op jit(solution)/shard_map/dot_general | solution.py:17
  2.6 0.0 copy-done
  2.6 1.4 %fusion.2 = f32[64,128]{1,0:T(8,128)S(1)} fusion(bf16[512,64]{0,1:T(8,128)(2,1)} %param.20, bf16[512,128]{1,0:T(8,128)(2,1)S(1)} %multiply_convert_fusion.1, bf16[512,512]{1,0:T(8,128)(2,1)S(1)} %copy-done, f32[512]{0:T(512)} %param.19), kind=kOutput, calls=%fused_computation.12 | convolution fusion | flops 75898880 | bytes 755712 | tf_op jit(solution)/shard_map/dot_general | solution.py:17
  4.0 0.7 %pad_maximum_fusion.2 = f32[81,128]{1,0:T(8,128)S(1)} fusion(f32[1,128]{1,0:T(1,128)S(1)} %convert_bitcast_fusion, f32[16,128]{1,0:T(8,128)} %param.21, f32[64,128]{1,0:T(8,128)S(1)} %fusion.2), kind=kLoop, calls=%fused_computation.70 | loop fusion | flops 20736 | bytes 82944 | tf_op jit(solution)/shard_map/concatenate | solution.py:138
  4.7 25.3 %all_gather.3 = f32[81,2048]{1,0:T(8,128)S(1)} all-gather(f32[81,128]{1,0:T(8,128)S(1)} %pad_maximum_fusion.2), channel_id=1, replica_groups=mesh['task'=2,'row'=4,'col'=4] {'row','col'}, dimensions={1}, use_global_device_ids=true | all-gather | bytes 705024 | tf_op jit(solution)/shard_map/all_gather | solution.py:139
  29.9 0.2 fusion.27
  30.2 0.1 slice.170
  30.3 0.1 fusion.3
  30.4 0.1 multiply_reduce_fusion
  31.1 5.7 %reduce-precision_convert_fusion = (bf16[2048,2048]{1,0:T(8,128)(2,1)S(1)}, bf16[2048,2048]{1,0:T(8,128)(2,1)S(1)}) fusion(f32[2048]{0:T(1024)S(1)} %multiply_reduce_fusion, f32[]{:T(128)} %bitcast.9, f32[81,2048]{1,0:T(8,128)S(1)} %all_gather.3), kind=kOutput, calls=%fused_computation.1 | convolution fusion | flops 570425344 | bytes 17055748 | tf_op jit(solution)/shard_map/while/body/eval_jaxpr/while/body/eval_jaxpr/dot_general | solution.py:17
  36.8 0.0 copy-start.1
  36.8 0.0 copy-start.3
  36.8 0.0 copy-start.4
  36.8 2.9 %fusion.5 = f32[128,2048]{1,0:T(8,128)S(1)} fusion(bf16[2048,2048]{1,0:T(8,128)(2,1)S(1)} %get-tuple-element.106, bf16[64,2048]{1,0:T(8,128)(2,1)S(1)} %get-tuple-element.132, bf16[64,2048]{1,0:T(8,128)(2,1)S(1)} %get-tuple-element.133), kind=kOutput, calls=%fused_computation.23 | convolution fusion | flops 1074790400 | bytes 9961472 | tf_op jit(solution)/shard_map/while/body/eval_jaxpr/while/body/eval_jaxpr/dot_general | solution.py:55
  39.7 2.7 %convolution_add_fusion.1 = f32[64,2048]{1,0:T(8,128)S(1)} fusion(bf16[64,2048]{1,0:T(8,128)(2,1)S(1)} %get-tuple-element.133, bf16[2048,2048]{1,0:T(8,128)(2,1)S(1)} %get-tuple-element.107, f32[128,2048]{1,0:T(8,128)S(1)} %fusion.5), kind=kOutput, calls=%fused_computation.5 | convolution fusion | flops 537133056 | bytes 10223616 | tf_op jit(solution)/shard_map/while/body/eval_jaxpr/while/body/eval_jaxpr/dot_general | solution.py:58
  42.4 0.0 copy-done.1
  42.4 0.1 copy-done.3
  43.2 0.0 copy-done.4
  43.2 0.1 convolution_add_fusion.5
  43.3 0.2 fusion.32
  43.5 0.1 fusion.19
  43.6 0.2 fusion.29
  43.8 0.1 copy.14
  43.9 1.5 %cholesky.59 = f32[16,16]{1,0:T(8,128)S(1)} custom-call(f32[16,16]{1,0:T(8,128)S(1)} %fusion.51), custom_call_target="Cholesky" | custom-call | tf_op jit(solution)/shard_map/jit(cholesky)/cholesky | solution.py:29
  45.5 0.6 compare_reduce_fusion.2
  46.1 0.6 fusion.34
  46.8 1.2 %custom-call.9 = f32[1,16,16]{1,2,0:T(8,128)S(1)} custom-call(f32[1,16,16]{2,1,0:T(8,128)S(1)} %fusion.34), custom_call_target="InvertDiagBlocksLowerTriangular" | custom-call | tf_op jit(solution)/shard_map/jit(_cho_solve)/triangular_solve | solution.py:29
  48.0 0.2 fusion.49
  48.2 0.1 fusion.47
  48.3 0.3 convolution_subtract_fusion
  48.7 0.2 fusion.60
  48.9 0.1 copy.15
  49.0 1.5 %cholesky.70 = f32[16,16]{1,0:T(8,128)S(1)} custom-call(f32[16,16]{1,0:T(8,128)S(1)} %fusion.46), custom_call_target="Cholesky" | custom-call | tf_op jit(solution)/shard_map/jit(cholesky)/cholesky | solution.py:29
  50.5 0.6 compare_reduce_fusion.1
  51.2 0.6 fusion.35
  51.8 1.2 %custom-call.10 = f32[1,16,16]{1,2,0:T(8,128)S(1)} custom-call(f32[1,16,16]{2,1,0:T(8,128)S(1)} %fusion.35), custom_call_target="InvertDiagBlocksLowerTriangular" | custom-call | tf_op jit(solution)/shard_map/jit(_cho_solve)/triangular_solve | solution.py:29
  53.1 0.0 copy-start.2
  53.1 0.2 fusion.44
  53.3 0.1 fusion.42
  53.4 0.4 broadcast_multiply_fusion.6
  53.8 0.1 fusion.4
  53.9 6.6 %fusion.9 = f32[128,2048]{1,0:T(8,128)S(1)} fusion(bf16[2048,2048]{1,0:T(8,128)(2,1)} %copy-done.3, bf16[64,2048]{1,0:T(8,128)(2,1)S(1)} %get-tuple-element.130, bf16[64,2048]{1,0:T(8,128)(2,1)S(1)} %get-tuple-element.131), kind=kOutput, calls=%fused_computation.28 | convolution fusion | flops 1074790400 | bytes 9961472 | tf_op jit(solution)/shard_map/while/body/eval_jaxpr/while/body/eval_jaxpr/dot_general | solution.py:55
  60.5 0.0 copy-done.2
  60.5 2.7 %convolution_add_fusion = f32[64,2048]{1,0:T(8,128)S(1)} fusion(bf16[64,2048]{1,0:T(8,128)(2,1)S(1)} %get-tuple-element.131, bf16[2048,2048]{1,0:T(8,128)(2,1)S(1)} %copy-done.2, f32[128,2048]{1,0:T(8,128)S(1)} %fusion.9), kind=kOutput, calls=%fused_computation.4 | convolution fusion | flops 537133056 | bytes 10223616 | tf_op jit(solution)/shard_map/while/body/eval_jaxpr/while/body/eval_jaxpr/dot_general | solution.py:58
  63.1 0.1 fusion.15
  63.2 0.2 fusion.61
  63.4 0.1 copy.16
  63.5 1.5 %cholesky.81 = f32[16,16]{1,0:T(8,128)S(1)} custom-call(f32[16,16]{1,0:T(8,128)S(1)} %fusion.41), custom_call_target="Cholesky" | custom-call | tf_op jit(solution)/shard_map/jit(cholesky)/cholesky | solution.py:29
  65.1 0.6 compare_reduce_fusion
  65.7 0.6 fusion.36
  66.4 1.2 %custom-call.11 = f32[1,16,16]{1,2,0:T(8,128)S(1)} custom-call(f32[1,16,16]{2,1,0:T(8,128)S(1)} %fusion.36), custom_call_target="InvertDiagBlocksLowerTriangular" | custom-call | tf_op jit(solution)/shard_map/jit(_cho_solve)/triangular_solve | solution.py:29
  67.6 0.2 fusion.39
  67.8 0.1 fusion.37
  68.0 0.3 fusion.63
  68.3 0.3 fusion.62
  68.6 0.3 fusion.25
  68.9 0.6 dynamic-slice_subtract_fusion
  (10 shorter events, 0.2 us)
Async XLA Ops:
  0.6 2.0 %copy-start = (bf16[512,512]{1,0:T(8,128)(2,1)S(1)}, bf16[512,512]{1,0:T(8,128)(2,1)}, u32[]{:S(2)}) copy-start(bf16[512,512]{1,0:T(8,128)(2,1)} %param.18) | copy-start | bytes 1572868
  36.8 5.6 %copy-start.1 = (bf16[2048,2048]{1,0:T(8,128)(2,1)}, bf16[2048,2048]{1,0:T(8,128)(2,1)S(1)}, u32[]{:S(2)}) copy-start(bf16[2048,2048]{1,0:T(8,128)(2,1)S(1)} %get-tuple-element.107) | copy-start | bytes 25165828
  36.8 5.7 %copy-start.3 = (bf16[2048,2048]{1,0:T(8,128)(2,1)}, bf16[2048,2048]{1,0:T(8,128)(2,1)S(1)}, u32[]{:S(2)}) copy-start(bf16[2048,2048]{1,0:T(8,128)(2,1)S(1)} %get-tuple-element.106) | copy-start | bytes 25165828
  36.8 6.3 %copy-start.4 = (f32[4,4]{1,0:T(4,128)S(1)}, f32[4,4]{1,0:T(4,128)}, u32[]{:S(2)}) copy-start(f32[4,4]{1,0:T(4,128)} %param.22) | copy-start | bytes 196
  53.1 7.4 %copy-start.2 = (bf16[2048,2048]{1,0:T(8,128)(2,1)S(1)}, bf16[2048,2048]{1,0:T(8,128)(2,1)}, u32[]{:S(2)}) copy-start(bf16[2048,2048]{1,0:T(8,128)(2,1)} %copy-done.1) | copy-start | bytes 25165828
where the time goes:
time: 69.9 us; the launch traced here: 69.6 us
  matrix products  27 us (39%)
  blocking collectives  25.3 us (36%)
  other arithmetic  14.6 us (21%)
  between operations  2.2 us (3%)
    all_gather x1, blocking collectives, on_device(): gathered = lax.all_gather(packed, ('row', 'col'), axis=1, tiled=True)  25.3 us
    dot_general x2, matrix products, split_product(): lax.dot_general(jnp.concatenate([d_high, d_low], axis=0), k_high, dims, p...  9.5 us
    dot_general x3, matrix products, left_product(): lax.dot_general(weights, values, (((0,), (0,)), ((), ())), preferred_elem...  8.27 us
    another operation x9, other arithmetic, solve_spd(): jnp.linalg.cholesky(matrix)  6.58 us
    another operation x6, other arithmetic, solve_spd(): jax.scipy.linalg.cho_solve((jnp.linalg.cholesky(matrix), True), right_side)  5.63 us
    dot_general x2, matrix products, split_product(): lax.dot_general(d_high, k_low, dims, preferred_element_type=jnp.float32)  5.32 us

commit v1 on v0

--- a/solution.py
+++ b/solution.py
@@ -136,7 +136,11 @@
     own_first = (lax.axis_index("row") * lax.axis_size("col") + lax.axis_index("col")) * own_count
     emb_rows = embedding.shape[0]
     packed = jnp.concatenate([embedding, targets, rung_value[None, :]], axis=0)
-    gathered = lax.all_gather(packed, ("row", "col"), axis=1, tiled=True)
+    size = lax.axis_size(("row", "col"))
+    repeats = [size if d == 1 else 1 for d in range(packed.ndim)]
+    gathered = lax.all_to_all(
+        jnp.tile(packed, repeats), ("row", "col"), split_axis=1, concat_axis=1, tiled=True
+    )
     all_embedding = gathered[:emb_rows].astype(jnp.bfloat16)
     all_targets = gathered[emb_rows : emb_rows + targets.shape[0]]
     all_rung = gathered[emb_rows + targets.shape[0]]

time: 69.9 us -> 69.2 us (0.990)
  blocking collectives: 25.3 us -> 0 us
  waiting for transfers between devices: 0 us -> 15.4 us
  starting transfers between devices: 0 us -> 7.39 us
  local copies, waits for them, and re-layouts: 0.51 us -> 1.34 us
  matrix products: 27 us -> 27.8 us
    all_gather x1 -> x0, blocking collectives: 25.3 us -> none  [on_device(): gathered = lax.all_gather(packed, ('row', 'col'), axis=1, tiled=True)]
    all_to_all x0 -> x1, waiting for transfers between devices: none -> 15.4 us  [on_device(): lax.all_to_all(jnp.tile(packed, repeats), ('row', 'col'), split_axis=1, c...]
    all_to_all x0 -> x1, starting transfers between devices: none -> 7.39 us  [on_device(): lax.all_to_all(jnp.tile(packed, repeats), ('row', 'col'), split_axis=1, c...]
    another operation x0 -> x1, local copies, waits for them, and re-layouts: none -> 0.9 us  [on_device(): jnp.tile(packed, repeats)]
    dot_general x1, matrix products: 0.13 us -> 0.88 us  [fidelity_matrix(): jnp.dot(lower, lower.T, precision=lax.Precision.HIGHEST)]
  transfers between devices with their start and end apart: 0 -> 1, of which waited for: 0 -> 1; matrix products, arithmetic and copies ran while one was open for 0% -> 1% of each run, Pallas kernels for 0% -> 0%
where the time goes in v1:
time: 69.2 us; the launch traced here: 68.8 us
  matrix products  27.8 us (40%)
  waiting for transfers between devices  15.4 us (22%)
  other arithmetic  14.6 us (21%)
  starting transfers between devices  7.39 us (11%)
  between operations  2.18 us (3%)
  local copies, waits for them, and re-layouts  1.34 us (2%)
    all_to_all x1, waiting for transfers between devices, on_device(): lax.all_to_all(jnp.tile(packed, repeats), ('row', 'col'), split_axis=1, c...  15.4 us
    dot_general x2, matrix products, split_product(): lax.dot_general(jnp.concatenate([d_high, d_low], axis=0), k_high, dims, p...  9.51 us
    dot_general x3, matrix products, left_product(): lax.dot_general(weights, values, (((0,), (0,)), ((), ())), preferred_elem...  8.3 us
    all_to_all x1, starting transfers between devices, on_device(): lax.all_to_all(jnp.tile(packed, repeats), ('row', 'col'), split_axis=1, c...  7.39 us
    another operation x9, other arithmetic, solve_spd(): jnp.linalg.cholesky(matrix)  6.52 us
    another operation x6, other arithmetic, solve_spd(): jax.scipy.linalg.cho_solve((jnp.linalg.cholesky(matrix), True), right_side)  5.63 us
    dot_general x2, matrix products, split_product(): lax.dot_general(d_high, k_low, dims, preferred_element_type=jnp.float32)  5.32 us
  transfers between devices with their start and end apart: 1, of which 1 were waited for; matrix products, arithmetic and copies ran while one was open for 1% of the time, Pallas kernels for 0%

profile of v1, /device:TPU:0, one launch (start us, length us, event | category | flops | bytes accessed | tf_op | source)
XLA Modules:
  0.0 68.8 jit_solution(6360241354419702214)
XLA Ops:
  0.6 0.0 copy-start
  0.6 0.7 %convert_bitcast_fusion = f32[1,128]{1,0:T(1,128)S(1)} fusion(s32[128]{0:T(128)} %param.15), kind=kLoop, calls=%fused_computation.124 | loop fusion | flops 128 | bytes 1024 | tf_op jit(solution)/shard_map/broadcast_in_dim | solution.py:138
  1.4 1.2 %multiply_convert_fusion.1 = bf16[512,128]{1,0:T(8,128)(2,1)S(1)} fusion(bf16[164,512]{1,0:T(8,128)(2,1)} %param.16, bf16[164,128]{1,0:T(8,128)(2,1)} %param.14, f32[512]{0:T(512)} %param.17), kind=kOutput, calls=%fused_computation.40 | convolution fusion | flops 21889024 | bytes 343040 | tf_op jit(solution)/shard_map/dot_general | solution.py:17
  2.6 0.0 copy-done
  2.6 1.4 %fusion.2 = f32[64,128]{1,0:T(8,128)S(1)} fusion(bf16[512,64]{0,1:T(8,128)(2,1)} %param.20, bf16[512,128]{1,0:T(8,128)(2,1)S(1)} %multiply_convert_fusion.1, bf16[512,512]{1,0:T(8,128)(2,1)S(1)} %copy-done, f32[512]{0:T(512)} %param.19), kind=kOutput, calls=%fused_computation.12 | convolution fusion | flops 75898880 | bytes 755712 | tf_op jit(solution)/shard_map/dot_general | solution.py:17
  4.0 0.7 %pad_maximum_fusion.2 = f32[81,128]{1,0:T(8,128)S(1)} fusion(f32[1,128]{1,0:T(1,128)S(1)} %convert_bitcast_fusion, f32[16,128]{1,0:T(8,128)} %param.21, f32[64,128]{1,0:T(8,128)S(1)} %fusion.2), kind=kLoop, calls=%fused_computation.81 | loop fusion | flops 20736 | bytes 82944 | tf_op jit(solution)/shard_map/concatenate | solution.py:138
  4.7 0.9 %tile.2 = f32[81,16,128]{2,0,1:T(8,128)} broadcast(f32[81,128]{1,0:T(8,128)S(1)} %pad_maximum_fusion.2), dimensions={0,2} | broadcast | bytes 705024 | tf_op jit(solution)/shard_map/tile | solution.py:142
  5.6 7.4 %all-to-all-start = ((f32[81,16,128]{2,0,1:T(8,128)}), f32[81,16,128]{2,0,1:T(8,128)S(1)}, u32[]{:S(2)}, u32[]{:S(2)}) async-start(f32[81,16,128]{2,0,1:T(8,128)} %tile.2), calls=%async_computation | async-start | bytes 1441792 | tf_op jit(solution)/shard_map/all_to_all | solution.py:141
  14.3 0.9 %convolution_add_fusion.5 = f32[4,4]{1,0:T(4,128)S(1)} fusion(f32[4,4]{1,0:T(4,128)} %param.22), kind=kOutput, calls=%fused_computation.14 | convolution fusion | flops 848 | bytes 128 | tf_op jit(solution)/shard_map/dot_general | solution.py:11
  15.2 15.4 %all-to-all-done = f32[81,16,128]{2,0,1:T(8,128)S(1)} async-done(((f32[81,16,128]{2,0,1:T(8,128)}), f32[81,16,128]{2,0,1:T(8,128)S(1)}, u32[]{:S(2)}, u32[]{:S(2)}) %all-to-all-start) | async-done | bytes 663584 | tf_op jit(solution)/shard_map/all_to_all | solution.py:141
  30.7 0.2 fusion.42
  30.9 0.1 fusion.3
  31.0 0.1 multiply_reduce_fusion
  31.1 5.7 %reduce-precision_convert_fusion = (bf16[2048,2048]{1,0:T(8,128)(2,1)S(1)}, bf16[2048,2048]{1,0:T(8,128)(2,1)S(1)}) fusion(f32[2048]{0:T(1024)S(1)} %bitcast.147, f32[]{:T(128)} %bitcast.9, f32[81,16,128]{2,0,1:T(8,128)S(1)} %all-to-all-done), kind=kOutput, calls=%fused_computation.1 | convolution fusion | flops 570425344 | bytes 17055748 | tf_op jit(solution)/shard_map/while/body/eval_jaxpr/while/body/eval_jaxpr/dot_general | solution.py:17
  36.8 0.0 copy-start.1
  36.8 0.0 copy-start.3
  36.8 2.9 %fusion.5 = f32[128,2048]{1,0:T(8,128)S(1)} fusion(bf16[2048,2048]{1,0:T(8,128)(2,1)S(1)} %get-tuple-element.106, bf16[64,2048]{1,0:T(8,128)(2,1)S(1)} %get-tuple-element.128, bf16[64,2048]{1,0:T(8,128)(2,1)S(1)} %get-tuple-element.129), kind=kOutput, calls=%fused_computation.24 | convolution fusion | flops 1074790400 | bytes 9961472 | tf_op jit(solution)/shard_map/while/body/eval_jaxpr/while/body/eval_jaxpr/dot_general | solution.py:55
  39.7 2.7 %convolution_add_fusion.1 = f32[64,2048]{1,0:T(8,128)S(1)} fusion(bf16[64,2048]{1,0:T(8,128)(2,1)S(1)} %get-tuple-element.129, bf16[2048,2048]{1,0:T(8,128)(2,1)S(1)} %get-tuple-element.107, f32[128,2048]{1,0:T(8,128)S(1)} %fusion.5), kind=kOutput, calls=%fused_computation.5 | convolution fusion | flops 537133056 | bytes 10223616 | tf_op jit(solution)/shard_map/while/body/eval_jaxpr/while/body/eval_jaxpr/dot_general | solution.py:58
  42.3 0.0 copy-done.1
  42.3 0.1 copy-done.3
  42.5 0.2 fusion.20
  42.8 0.1 copy.21
  42.9 1.5 %cholesky.59 = f32[16,16]{1,0:T(8,128)S(1)} custom-call(f32[16,16]{1,0:T(8,128)S(1)} %fusion.61), custom_call_target="Cholesky" | custom-call | tf_op jit(solution)/shard_map/jit(cholesky)/cholesky | solution.py:29
  44.4 0.6 compare_reduce_fusion.2
  45.1 0.6 fusion.44
  45.7 1.2 %custom-call.9 = f32[1,16,16]{1,2,0:T(8,128)S(1)} custom-call(f32[1,16,16]{2,1,0:T(8,128)S(1)} %fusion.44), custom_call_target="InvertDiagBlocksLowerTriangular" | custom-call | tf_op jit(solution)/shard_map/jit(_cho_solve)/triangular_solve | solution.py:29
  46.9 0.2 convolution_bitcast_fusion
  47.2 0.1 copy.22
  47.3 0.3 fusion.59
  47.5 0.1 fusion.57
  47.7 0.3 convolution_subtract_fusion
  48.0 0.2 fusion.70
  48.2 0.1 fusion.56
  48.3 1.5 %cholesky.70 = f32[16,16]{1,0:T(8,128)S(1)} custom-call(f32[16,16]{1,0:T(8,128)S(1)} %fusion.56), custom_call_target="Cholesky" | custom-call | tf_op jit(solution)/shard_map/jit(cholesky)/cholesky | solution.py:29
  49.8 0.6 compare_reduce_fusion.1
  50.4 0.6 fusion.45
  51.1 1.2 %custom-call.10 = f32[1,16,16]{1,2,0:T(8,128)S(1)} custom-call(f32[1,16,16]{2,1,0:T(8,128)S(1)} %fusion.45), custom_call_target="InvertDiagBlocksLowerTriangular" | custom-call | tf_op jit(solution)/shard_map/jit(_cho_solve)/triangular_solve | solution.py:29
  52.3 0.0 copy-start.2
  52.3 0.2 fusion.54
  52.5 0.1 fusion.52
  52.6 0.4 broadcast_multiply_fusion.3
  53.0 0.1 fusion.4
  53.1 6.6 %fusion.9 = f32[128,2048]{1,0:T(8,128)S(1)} fusion(bf16[2048,2048]{1,0:T(8,128)(2,1)} %copy-done.3, bf16[64,2048]{1,0:T(8,128)(2,1)S(1)} %get-tuple-element.108, bf16[64,2048]{1,0:T(8,128)(2,1)S(1)} %get-tuple-element.109), kind=kOutput, calls=%fused_computation.29 | convolution fusion | flops 1074790400 | bytes 9961472 | tf_op jit(solution)/shard_map/while/body/eval_jaxpr/while/body/eval_jaxpr/dot_general | solution.py:55
  59.7 0.0 copy-done.2
  59.7 2.7 %convolution_add_fusion = f32[64,2048]{1,0:T(8,128)S(1)} fusion(bf16[64,2048]{1,0:T(8,128)(2,1)S(1)} %get-tuple-element.109, bf16[2048,2048]{1,0:T(8,128)(2,1)S(1)} %copy-done.2, f32[128,2048]{1,0:T(8,128)S(1)} %fusion.9), kind=kOutput, calls=%fused_computation.4 | convolution fusion | flops 537133056 | bytes 10223616 | tf_op jit(solution)/shard_map/while/body/eval_jaxpr/while/body/eval_jaxpr/dot_general | solution.py:58
  62.4 0.1 fusion.26
  62.5 0.2 fusion.71
  62.7 0.1 copy.23
  62.8 1.5 %cholesky.81 = f32[16,16]{1,0:T(8,128)S(1)} custom-call(f32[16,16]{1,0:T(8,128)S(1)} %fusion.51), custom_call_target="Cholesky" | custom-call | tf_op jit(solution)/shard_map/jit(cholesky)/cholesky | solution.py:29
  64.3 0.6 compare_reduce_fusion
  65.0 0.6 fusion.46
  65.6 1.2 %custom-call.11 = f32[1,16,16]{1,2,0:T(8,128)S(1)} custom-call(f32[1,16,16]{2,1,0:T(8,128)S(1)} %fusion.46), custom_call_target="InvertDiagBlocksLowerTriangular" | custom-call | tf_op jit(solution)/shard_map/jit(_cho_solve)/triangular_solve | solution.py:29
  66.9 0.2 fusion.49
  67.1 0.1 fusion.47
  67.2 0.3 fusion.73
  67.5 0.3 fusion.72
  67.9 0.3 fusion.18
  68.2 0.6 dynamic-slice_subtract_fusion
  (11 shorter events, 0.3 us)
Async XLA Ops:
  0.6 2.0 %copy-start = (bf16[512,512]{1,0:T(8,128)(2,1)S(1)}, bf16[512,512]{1,0:T(8,128)(2,1)}, u32[]{:S(2)}) copy-start(bf16[512,512]{1,0:T(8,128)(2,1)} %param.18) | copy-start | bytes 1572868
  5.6 25.0 %all-to-all-start = ((f32[81,16,128]{2,0,1:T(8,128)}), f32[81,16,128]{2,0,1:T(8,128)S(1)}, u32[]{:S(2)}, u32[]{:S(2)}) async-start(f32[81,16,128]{2,0,1:T(8,128)} %tile.2), calls=%async_computation | async-start | bytes 1441792 | tf_op jit(solution)/shard_map/all_to_all | solution.py:141
  36.8 5.6 %copy-start.1 = (bf16[2048,2048]{1,0:T(8,128)(2,1)}, bf16[2048,2048]{1,0:T(8,128)(2,1)S(1)}, u32[]{:S(2)}) copy-start(bf16[2048,2048]{1,0:T(8,128)(2,1)S(1)} %get-tuple-element.107) | copy-start | bytes 25165828
  36.8 5.7 %copy-start.3 = (bf16[2048,2048]{1,0:T(8,128)(2,1)}, bf16[2048,2048]{1,0:T(8,128)(2,1)S(1)}, u32[]{:S(2)}) copy-start(bf16[2048,2048]{1,0:T(8,128)(2,1)S(1)} %get-tuple-element.106) | copy-start | bytes 25165828
  52.3 7.4 %copy-start.2 = (bf16[2048,2048]{1,0:T(8,128)(2,1)S(1)}, bf16[2048,2048]{1,0:T(8,128)(2,1)}, u32[]{:S(2)}) copy-start(bf16[2048,2048]{1,0:T(8,128)(2,1)} %copy-done.1) | copy-start | bytes 25165828
